TPU v7x, 32 devices: a whole 2x2x4 slice. The times are simulated.
32 devices in a mesh: groups: 2 (over y), seq: 4 (over z), tensor: 4 (over x, core).
Axes of the slice: x: 2, y: 2, z: 4, core: 2. Of those that a mesh axis runs over, the one named last changes fastest.
Arguments:
- x_in: bfloat16 [4096, 5120], P(('groups', 'seq'), 'tensor'), parts along dimension 0, may hold values from -6 to 6
- z_gate: bfloat16 [4096, 5120], P(('groups', 'seq'), 'tensor'), parts along dimension 0, may hold values from -32 to 32
- bc_in: bfloat16 [4096, 256], P(('groups', 'seq')), parts along dimension 0, may hold values from -6 to 6
- step_size: float32 [80, 4096], P('tensor', ('groups', 'seq')), parts along dimension 1, may hold values from 0 to 0.4
- log_keep: float32 [80, 4096], P('tensor', ('groups', 'seq')), parts along dimension 1, may hold values from -1 to 0
- skip_gain: float32 [80], P('tensor'), may hold values from 0.5 to 2
- conv_x: bfloat16 [4, 5120], P(None, 'tensor'), may hold values from -3 to 3
- conv_bc: bfloat16 [4, 256], replicated, may hold values from -3 to 3
- norm_gain: float32 [5120], P('tensor'), may hold values from 0.1 to 1.9
- seg_ends: int32 [1024], P(('groups', 'seq')), parts along dimension 0, may hold values from 0 to 2047, as said below
- pool_query: bfloat16 [320, 5120], P(('groups', 'seq'), 'tensor'), parts along dimension 0, may hold values from -64 to 64
- pool_start: int32 [320], P(('groups', 'seq')), parts along dimension 0, may hold values from 0 to 255, as said below
- pool_stop: int32 [320], P(('groups', 'seq')), parts along dimension 0, may hold values from 64 to 512
Outputs:
- mixed_seq: bfloat16 [4096, 5120], P(('groups', 'seq'), 'tensor'), parts along dimension 0
- pooled: float32 [320, 5120], P(('groups', 'seq'), 'tensor'), parts along dimension 0
There are 2 independent parts, one for each index of `groups`. A program takes and returns all parts, laid end to end along the dimension named above; an argument that names none is the same for every part. Nothing has to cross between parts.
Inputs may be any that keep to these rules, and one draw needn't show every extreme that they name: The tokens fall into blocks of 512; block b holds exactly the 128 segment ends seg_ends[b * 128] to seg_ends[(b + 1) * 128 - 1], strictly increasing. pool_start < pool_stop for every pooled row.
All inputs are finite; a program needn't handle non-finite values.
Results may differ from a plain program's by a relative error of at most 0.039.
Values may be sent and summed in bfloat16 or wider, within the bound.
No kernel may reach another device: no remote copies, remote signals or barrier semaphores. Data moves between devices by JAX's collectives and lax.ppermute only.
A program may use at most 64 MiB of HBM per device.

v0:
```python
import math
import jax
import jax.numpy as jnp
from jax import lax
from jax.sharding import PartitionSpec as P

STRETCH = 256
POOL_HEADS = 32
EPSILON = 1e-05
MASKED = -1e30


def passed_along(value, axis, steps):
    count = lax.axis_size(axis)
    leading, last = (max(0, -steps), min(count, count - steps))
    return lax.ppermute(value, axis, [(source, source + steps) for source in range(leading, last)])


def prefix(part, axis, combine, identity):
    place = lax.axis_index(axis)
    gathered = jax.tree.map(lambda a: lax.all_gather(a, axis), part)
    state = jax.tree.map(lambda a, e: jnp.zeros_like(a) + jnp.asarray(e, a.dtype), part, identity)

    def one(lap, state):
        return combine(
            state, jax.tree.map(lambda a: lax.dynamic_index_in_dim(a, lap, 0, False), gathered)
        )

    return lax.fori_loop(0, place, one, state)


def silu_act(values):
    return values / (1.0 + jnp.exp(-values))


def causal_conv(before, current, weights):
    kernel_width = weights.shape[0]
    length = current.shape[0]
    padded = jnp.concatenate([before, current], axis=0)
    summed = jnp.zeros(current.shape, jnp.float32)
    for offset in range(kernel_width):
        summed = summed + padded[offset : offset + length].astype(jnp.float32) * weights[
            offset
        ].astype(jnp.float32)
    return silu_act(summed).astype(jnp.bfloat16)


def stretch_local(x_block, b_block, c_block, step_block, keep_block):
    block_len = x_block.shape[0]
    cumul_keep = jnp.cumsum(keep_block, axis=1)
    lower_mask = lax.broadcasted_iota(jnp.int32, (block_len, block_len), 0) >= lax.broadcasted_iota(
        jnp.int32, (block_len, block_len), 1
    )
    inner_prod = jnp.einsum("is,js->ij", c_block, b_block, preferred_element_type=jnp.float32)
    spread = cumul_keep[:, :, None] - cumul_keep[:, None, :]
    decay_mask = jnp.where(lower_mask[None], jnp.exp(jnp.where(lower_mask[None], spread, 0.0)), 0.0)
    mixing = (decay_mask * inner_prod[None] * step_block[:, None, :]).astype(jnp.bfloat16)
    intra_part = jnp.einsum("hij,jhp->ihp", mixing, x_block, preferred_element_type=jnp.float32)
    tail_weight = jnp.exp(cumul_keep[:, -1:] - cumul_keep) * step_block
    weighted = (tail_weight.T[:, :, None] * x_block.astype(jnp.float32)).astype(jnp.bfloat16)
    stretch_state = jnp.einsum("jhp,js->hps", weighted, b_block, preferred_element_type=jnp.float32)
    return (intra_part, stretch_state, cumul_keep)


def combine(earlier, later):
    return (earlier[0] * jnp.exp(later[1])[:, None, None] + later[0], earlier[1] + later[1])


def read_state(c_block, state_in):
    state_high = state_in.astype(jnp.bfloat16)
    state_low = (state_in - state_high.astype(jnp.float32)).astype(jnp.bfloat16)
    high_part = jnp.einsum("is,hps->ihp", c_block, state_high, preferred_element_type=jnp.float32)
    low_part = jnp.einsum("is,hps->ihp", c_block, state_low, preferred_element_type=jnp.float32)
    return high_part + low_part


def local(
    x_in,
    z_gate,
    bc_in,
    step_size,
    log_keep,
    skip_gain,
    conv_x,
    conv_bc,
    norm_gain,
    seg_ends,
    pool_query,
    pool_start,
    pool_stop,
):
    tok_rows = x_in.shape[0]
    channels = x_in.shape[1]
    heads_local = step_size.shape[0]
    head_width = channels // heads_local
    state_width = bc_in.shape[1] // 2
    rim_rows = conv_x.shape[0] - 1
    edge_rows = jnp.concatenate([x_in[tok_rows - rim_rows :], bc_in[tok_rows - rim_rows :]], axis=1)
    before = passed_along(edge_rows, "seq", 1)
    x_conv = causal_conv(before[:, :channels], x_in, conv_x)
    bc_conv = causal_conv(before[:, channels:], bc_in, conv_bc)
    b_mat = bc_conv[:, :state_width]
    c_mat = bc_conv[:, state_width:]
    x_heads = x_conv.reshape(tok_rows, heads_local, head_width)
    stretch_count = tok_rows // STRETCH
    entry_state = jnp.zeros((heads_local, head_width, state_width), jnp.float32)
    decay_total = jnp.zeros((heads_local,), jnp.float32)
    saved_parts = []
    for block_index in range(stretch_count):
        first_row = block_index * STRETCH
        last_row = first_row + STRETCH
        intra_part, stretch_state, cumul_keep = stretch_local(
            x_heads[first_row:last_row],
            b_mat[first_row:last_row],
            c_mat[first_row:last_row],
            step_size[:, first_row:last_row],
            log_keep[:, first_row:last_row],
        )
        saved_parts.append((intra_part, cumul_keep, entry_state, decay_total))
        entry_state = jnp.exp(cumul_keep[:, -1])[:, None, None] * entry_state + stretch_state
        decay_total = decay_total + cumul_keep[:, -1]
    incoming, unused = prefix(
        (entry_state, decay_total),
        "seq",
        combine,
        (jnp.zeros_like(entry_state), jnp.zeros_like(decay_total)),
    )
    pieces_out = []
    for block_index in range(stretch_count):
        intra_part, cumul_keep, entry_part, decay_part = saved_parts[block_index]
        first_row = block_index * STRETCH
        state_in = entry_part + jnp.exp(decay_part)[:, None, None] * incoming
        from_state = read_state(c_mat[first_row : first_row + STRETCH], state_in)
        pieces_out.append(intra_part + jnp.exp(cumul_keep).T[:, :, None] * from_state)
    ssd_out = jnp.concatenate(pieces_out, axis=0) + skip_gain[None, :, None] * x_heads.astype(
        jnp.float32
    )
    gated = ssd_out.reshape(tok_rows, channels) * silu_act(z_gate.astype(jnp.float32))
    square_sum = lax.psum(jnp.sum(gated * gated, axis=1), "tensor")
    width_all = channels * lax.axis_size("tensor")
    mixed_seq = (
        gated * lax.rsqrt(square_sum / width_all + EPSILON)[:, None] * norm_gain[None, :]
    ).astype(jnp.bfloat16)
    local_ends = seg_ends - lax.axis_index("seq") * tok_rows
    summaries = jnp.take(mixed_seq, local_ends, axis=0)
    pool_heads_local = POOL_HEADS // lax.axis_size("tensor")
    pool_width = channels // pool_heads_local
    scale_factor = 1.0 / math.sqrt(pool_width)
    pools_local = pool_query.shape[0]
    queries = pool_query.reshape(pools_local, pool_heads_local, pool_width)
    piece = lax.all_gather(summaries, "seq", axis=0, tiled=True)
    peak = jnp.full((pool_heads_local, pools_local), MASKED, jnp.float32)
    numer = jnp.zeros((pools_local, pool_heads_local, pool_width), jnp.float32)
    count = piece.shape[0]
    seg_index = lax.iota(jnp.int32, count)
    inside = (seg_index[None, :] >= pool_start[:, None]) & (seg_index[None, :] < pool_stop[:, None])
    keys_block = piece.reshape(count, pool_heads_local, pool_width)
    logits = (
        jnp.einsum("pad,rad->apr", queries, keys_block, preferred_element_type=jnp.float32)
        * scale_factor
    )
    logits = jnp.where(inside[None], logits, MASKED)
    new_peak = jnp.maximum(peak, jnp.max(logits, axis=2))
    expo = jnp.where(inside[None], jnp.exp(logits - new_peak[:, :, None]), 0.0)
    rescale = jnp.exp(peak - new_peak)
    denom = jnp.sum(expo, axis=2)
    numer = numer * rescale.T[:, :, None] + jnp.einsum(
        "apr,rad->pad", expo.astype(jnp.bfloat16), keys_block, preferred_element_type=jnp.float32
    )
    peak, denom, numer = (new_peak, denom, numer)
    pooled = (numer / denom.T[:, :, None]).reshape(pools_local, channels)
    return (mixed_seq, pooled)


def solution(mesh):
    in_specs = (
        P(("groups", "seq"), "tensor"),
        P(("groups", "seq"), "tensor"),
        P(("groups", "seq"), None),
        P("tensor", ("groups", "seq")),
        P("tensor", ("groups", "seq")),
        P("tensor"),
        P(None, "tensor"),
        P(),
        P("tensor"),
        P(("groups", "seq")),
        P(("groups", "seq"), "tensor"),
        P(("groups", "seq")),
        P(("groups", "seq")),
    )
    out_specs = (P(("groups", "seq"), "tensor"), P(("groups", "seq"), "tensor"))
    return jax.shard_map(local, mesh=mesh, in_specs=in_specs, out_specs=out_specs, check_vma=False)
```

profile of v0, /device:TPU:0, one launch (start us, length us, event | category | flops | bytes accessed | tf_op | source)
XLA Modules:
  0.0 157.4 jit_solution(5044019205403970520)
XLA Ops:
  7.2 0.7 slice.120
  7.9 0.7 slice.121
  8.7 5.0 %collective-permute-start = (bf16[3,1536]{1,0:T(4,128)(2,1)S(1)}, bf16[3,1536]{1,0:T(4,128)(2,1)S(1)}, u32[]{:S(2)}, u32[]{:S(2)}) collective-permute-start(bf16[3,1536]{1,0:T(4,128)(2,1)S(1)} %pad_maximum_fusion.2), channel_id=1, source_target_pairs={{0,4},{4,8},{8,12},{1,5},{5,9},{9,13},{2,6},{6,10},{10,14},{3,7},{... | collective-permute-start | bytes 27656 | tf_op jit(solution)/shard_map/ppermute | solution.py:16
  13.6 0.8 fusion.71
  14.4 0.6 reduce-window.14
  15.4 0.6 reduce-window.16
  16.3 0.8 slice_convert_fusion.3
  17.2 0.8 slice_reduce_fusion.2
  17.9 0.5 fusion.72
  18.5 1.5 fusion.70
  19.9 0.9 convert_reduce_fusion.3
  20.8 0.6 exp.65
  21.5 4.0 %divide_convert_fusion = bf16[512,1280]{1,0:T(8,128)(2,1)S(1)} fusion(bf16[512,1280]{1,0:T(8,128)(2,1)} %param.15, bf16[3,1280]{1,0:T(4,128)(2,1)S(1)} %slice.158, f32[1280]{0:T(1024)S(1)} %get-tuple-element.52, f32[1280]{0:T(1024)S(1)} %get-tuple-element.53, f32[1280]{0:T(1024)S(1)} %get-tuple-element.51, f32[1280]{0:T(1024)S(1)} %get-tuple-element.50), kind=kLoop, calls=%fused_computation.25 | loop fusion | flops 15728640 | bytes 2649600 | tf_op jit(solution)/shard_map/convert_element_type | solution.py:45
  25.6 0.2 copy.34
  25.8 0.2 copy.39
  26.1 1.9 %divide_convert_fusion.1 = bf16[512,256]{1,0:T(8,128)(2,1)S(1)} fusion(bf16[512,256]{1,0:T(8,128)(2,1)} %param.17, bf16[3,256]{1,0:T(4,128)(2,1)S(1)} %slice.165, f32[256]{0:T(256)S(1)} %bitcast.90, f32[256]{0:T(256)S(1)} %bitcast.91, f32[256]{0:T(256)S(1)} %bitcast.89, f32[256]{0:T(256)S(1)} %bitcast.88), kind=kLoop, calls=%fused_computation.59 | loop fusion | flops 3145728 | bytes 529920 | tf_op jit(solution)/shard_map/convert_element_type | solution.py:45
  28.0 1.1 convolution_add_fusion.3
  29.1 1.9 %convolution_add_fusion.2 = f32[20,64,128]{2,1,0:T(8,128)} fusion(bf16[256,20,64]{0,2,1:T(8,128)(2,1)S(1)} %bitcast.75, f32[256,20]{0,1:T(8,128)} %get-tuple-element.72, f32[20,64,128]{2,1,0:T(8,128)S(1)} %convolution_add_fusion.3, f32[20]{0:T(128)} %exp.65, bf16[512,256]{1,0:T(8,128)(2,1)S(1)} %divide_convert_fusion.1), kind=kOutput, calls=%fused_computation.43 | convolution fusion | flops 85196800 | bytes 2052176 | tf_op jit(solution)/shard_map/jhp,js->hps/dot_general | solution.py:61
  31.1 1.2 dynamic-slice
  33.0 0.9 dynamic-update-slice
  33.8 10.1 %all-reduce = f32[80]{0:T(128)S(1)} all-reduce(f32[80]{0:T(128)S(1)} %dynamic-update-slice), channel_id=2, replica_groups=mesh['groups'=2,'seq'=4,'tensor'=4] {'seq'}, use_global_device_ids=true, to_apply=%add | all-reduce | flops 80 | bytes 640
  44.1 0.7 mul.319
  44.8 0.7 mul.320
  45.4 0.7 compare_and_fusion
  46.5 3.7 %fusion.18 = f32[256,20,64]{0,2,1:T(8,128)} fusion(bf16[256,20,64]{0,2,1:T(8,128)(2,1)S(1)} %bitcast.78, f32[20,256]{1,0:T(8,128)} %get-tuple-element.70, f32[256,256]{1,0:T(8,128)S(1)} %fusion.57, f32[20,256]{1,0:T(8,128)} %bitcast.81, pred[256,256]{1,0:T(8,128)(4,1)S(1)} %iota_compare_fusion), kind=kOutput, calls=%fused_computation.31 | convolution fusion | flops 175636480 | bytes 2334720 | tf_op jit(solution)/shard_map/hij,jhp->ihp/dot_general | solution.py:58
  50.3 2.9 %fusion.17 = f32[256,20,64]{0,2,1:T(8,128)} fusion(bf16[256,20,64]{0,2,1:T(8,128)(2,1)S(1)} %bitcast.76, f32[20,256]{1,0:T(8,128)S(1)} %copy-done.11, f32[256,256]{1,0:T(8,128)S(1)} %fusion.53, f32[20,256]{1,0:T(8,128)S(1)} %bitcast.84, pred[256,256]{1,0:T(8,128)(4,1)S(1)} %iota_compare_fusion), kind=kOutput, calls=%fused_computation.30 | convolution fusion | flops 175636480 | bytes 2334720 | tf_op jit(solution)/shard_map/hij,jhp->ihp/dot_general | solution.py:58
  53.1 33.0 %all-gather.7.cloned.1.call-done = f32[80,64,128]{2,1,0:T(8,128)} async-done(((f32[20,64,128]{2,1,0:T(8,128)}), f32[80,64,128]{2,1,0:T(8,128)}) %all-gather.7.cloned.1.call-update) | async-done | bytes 2621456 | tf_op jit(solution)/shard_map/all_gather | solution.py:21
  86.3 0.3 fusion.44
  86.6 0.4 copy-done.9
  87.0 0.6 copy-done.3
  87.6 1.4 fusion.21
  89.0 2.8 %copy.40 = f32[256,1280]{1,0:T(8,128)} copy(f32[256,1280]{0,1:T(8,128)} %bitcast.73) | data formatting | bytes 2621440 | tf_op jit(solution)/shard_map/concatenate | solution.py:135
  91.8 0.4 fusion.41
  92.2 0.9 copy-done.2
  93.1 1.4 fusion.22
  94.6 2.9 %copy.41 = f32[256,1280]{1,0:T(8,128)} copy(f32[256,1280]{0,1:T(8,128)} %bitcast.72) | data formatting | bytes 2621440 | tf_op jit(solution)/shard_map/concatenate | solution.py:135
  97.5 4.2 %multiply_reduce_fusion = (f32[512]{0:T(512)S(1)}, f32[512,1280]{1,0:T(8,128)}) fusion(bf16[512,1280]{1,0:T(8,128)(2,1)} %param.16, bf16[512,1280]{1,0:T(8,128)(2,1)S(1)} %divide_convert_fusion, f32[1280]{0:T(1024)S(1)} %copy-done.10, f32[256,1280]{1,0:T(8,128)} %copy.41, f32[256,1280]{1,0:T(8,128)S(1)} %copy-done.1), kind=kLoop, calls=%fused_computation.14 | loop fusion | flops 7208448 | bytes 7871488 | tf_op jit(solution)/shard_map/reduce_sum | solution.py:139
  101.7 6.4 %psum.7 = f32[512]{0:T(512)S(1)} all-reduce(f32[512]{0:T(512)S(1)} %get-tuple-element.66), channel_id=1, replica_groups=mesh['groups'=2,'seq'=4,'tensor'=4] {'tensor'}, use_global_device_ids=true, to_apply=%region_7.8 | all-reduce | flops 512 | bytes 4096 | tf_op jit(solution)/shard_map/psum | solution.py:139
  108.1 2.0 %multiply_convert_fusion.4 = bf16[512,1280]{1,0:T(8,128)(2,1)S(1)} fusion(f32[512,1280]{1,0:T(8,128)} %get-tuple-element.67, f32[1280]{0:T(1024)S(1)} %copy-done.12, f32[512]{0:T(512)S(1)} %add_rsqrt_fusion), kind=kLoop, calls=%fused_computation.13 | loop fusion | flops 1966080 | bytes 3939328 | tf_op jit(solution)/shard_map/convert_element_type | solution.py:143
  110.2 0.9 gather_fusion
  111.1 0.8 broadcast_select_fusion
  112.0 0.2 reshape.192
  112.3 34.4 %all-gather.5.cloned.1.call-done = bf16[512,1280]{1,0:T(8,128)(2,1)} async-done(((bf16[128,1280]{1,0:T(8,128)(2,1)}), bf16[512,1280]{1,0:T(8,128)(2,1)}) %all-gather.5.cloned.1.call-update) | async-done | bytes 1310736 | tf_op jit(solution)/shard_map/all_gather | solution.py:151
  146.7 1.6 %copy.42 = bf16[512,1280]{0,1:T(8,128)(2,1)S(1)} copy(bf16[512,1280]{1,0:T(8,128)(2,1)} %all-gather.5.cloned.1.call-done) | data formatting | bytes 2621440 | tf_op jit(solution)/shard_map/all_gather | solution.py:151
  148.3 0.4 fusion.73
  148.7 0.3 fusion.31
  149.0 0.6 fusion.28
  149.7 0.8 reshape.193
  (68 shorter events, 1.7 us)
Async XLA Ops:
  7.2 79.0 %all-gather.7.cloned.1.call-start = ((), (), s32[]{:S(2)}) async-start(), calls=%async_computation.1 | async-start | bytes 3276800 | tf_op jit(solution)/shard_map/all_gather | solution.py:21
  8.7 12.8 %collective-permute-start = (bf16[3,1536]{1,0:T(4,128)(2,1)S(1)}, bf16[3,1536]{1,0:T(4,128)(2,1)S(1)}, u32[]{:S(2)}, u32[]{:S(2)}) collective-permute-start(bf16[3,1536]{1,0:T(4,128)(2,1)S(1)} %pad_maximum_fusion.2), channel_id=1, source_target_pairs={{0,4},{4,8},{8,12},{1,5},{5,9},{9,13},{2,6},{6,10},{10,14},{3,7},{... | collective-permute-start | bytes 27656 | tf_op jit(solution)/shard_map/ppermute | solution.py:16
  15.3 6.1 %copy-start.4 = (f32[3,8,2,128]{3,1,2,0:T(8,128)}, f32[3,8,2,128]{3,1,2,0:T(8,128)S(1)}, u32[]{:S(2)}) copy-start(f32[3,8,2,128]{3,1,2,0:T(8,128)S(1)} %copy.45) | copy-start | bytes 73732
  16.3 5.1 %copy-start.5 = (f32[3,8,2,128]{3,1,2,0:T(8,128)}, f32[3,8,2,128]{3,1,2,0:T(8,128)S(1)}, u32[]{:S(2)}) copy-start(f32[3,8,2,128]{3,1,2,0:T(8,128)S(1)} %copy.46) | copy-start | bytes 73732
  31.0 115.7 %all-gather.5.cloned.1.call-start = ((), (), s32[]{:S(2)}) async-start(), calls=%async_computation | async-start | bytes 1638400 | tf_op jit(solution)/shard_map/all_gather | solution.py:151
  46.5 3.7 %copy-start.6 = (f32[3,8,2,128]{3,1,2,0:T(8,128)S(1)}, f32[3,8,2,128]{3,1,2,0:T(8,128)}, u32[]{:S(2)}) copy-start(f32[3,8,2,128]{3,1,2,0:T(8,128)} %copy-done.5) | copy-start | bytes 73732
  46.5 3.7 %copy-start.11 = (f32[20,256]{1,0:T(8,128)S(1)}, f32[20,256]{1,0:T(8,128)}, u32[]{:S(2)}) copy-start(f32[20,256]{1,0:T(8,128)} %get-tuple-element.73) | copy-start | bytes 61444
  86.3 0.7 copy-start.9
  86.3 1.3 copy-start.3
  87.6 4.2 %copy-start.13 = (f32[20]{0:T(128)S(1)}, f32[20]{0:T(128)}, u32[]{:S(2)}) copy-start(f32[20]{0:T(128)} %get-tuple-element.84) | copy-start | bytes 244
  89.0 3.2 %copy-start.8 = (f32[256,20]{0,1:T(8,128)S(1)}, f32[256,20]{0,1:T(8,128)}, u32[]{:S(2)}) copy-start(f32[256,20]{0,1:T(8,128)} %get-tuple-element.76) | copy-start | bytes 61444
  91.8 1.3 copy-start.2
  94.6 2.9 %copy-start.1 = (f32[256,1280]{1,0:T(8,128)S(1)}, f32[256,1280]{1,0:T(8,128)}, u32[]{:S(2)}) copy-start(f32[256,1280]{1,0:T(8,128)} %copy.40) | copy-start | bytes 3932164
  94.6 2.9 %copy-start.10 = (f32[1280]{0:T(1024)S(1)}, f32[1280]{0:T(1024)}, u32[]{:S(2)}) copy-start(f32[1280]{0:T(1024)} %mul.320) | copy-start | bytes 15364
  97.5 10.6 %copy-start.12 = (f32[1280]{0:T(1024)S(1)}, f32[1280]{0:T(1024)}, u32[]{:S(2)}) copy-start(f32[1280]{0:T(1024)} %param.23) | copy-start | bytes 15364
  110.1 38.2 %copy-start = (bf16[512,1280]{1,0:T(8,128)(2,1)}, bf16[512,1280]{1,0:T(8,128)(2,1)S(1)}, u32[]{:S(2)}) copy-start(bf16[512,1280]{1,0:T(8,128)(2,1)S(1)} %multiply_convert_fusion.4) | copy-start | bytes 3932164
  110.2 1.8 %copy-start.7 = (bf16[40,1280]{1,0:T(8,128)(2,1)S(1)}, bf16[40,1280]{1,0:T(8,128)(2,1)}, u32[]{:S(2)}) copy-start(bf16[40,1280]{1,0:T(8,128)(2,1)} %param.25) | copy-start | bytes 307204
  110.2 2.0 %copy-start.14 = (s32[40]{0:T(128)S(1)}, s32[40]{0:T(128)}, u32[]{:S(2)}) copy-start(s32[40]{0:T(128)} %param.27) | copy-start | bytes 484
  110.2 2.0 %copy-start.15 = (s32[40]{0:T(128)S(1)}, s32[40]{0:T(128)}, u32[]{:S(2)}) copy-start(s32[40]{0:T(128)} %param.26) | copy-start | bytes 484
Sparse Core Ops, SparseCore 0:
  31.1 55.0 all-gather.6
  112.1 34.5 all-gather.4
where the time goes:
time: 158 us; the launch traced here: 157 us
  waiting for transfers between devices  67.5 us (43%)
  other arithmetic  20 us (13%)
  local copies, waits for them, and re-layouts  18.7 us (12%)
  blocking collectives  16.5 us (10%)
  between operations  15.1 us (10%)
  matrix products  14.5 us (9%)
  starting transfers between devices  5.04 us (3%)
    all_gather x1, waiting for transfers between devices, local(): piece = lax.all_gather(summaries, 'seq', axis=0, tiled=True)  34.4 us
    all_gather x1, waiting for transfers between devices, prefix(): gathered = jax.tree.map(lambda a: lax.all_gather(a, axis), part)  33 us
    unnamed x1, blocking collectives  10.1 us
    dot_general x2, matrix products, stretch_local(): jnp.einsum('hij,jhp->ihp', mixing, x_block, preferred_element_type=jnp.fl...  6.59 us
    psum x1, blocking collectives, local(): square_sum = lax.psum(jnp.sum(gated * gated, axis=1), 'tensor')  6.37 us
    convert_element_type x2, other arithmetic, causal_conv(): return silu_act(summed).astype(jnp.bfloat16)  5.91 us
    concatenate x2, local copies, waits for them, and re-layouts, local(): jnp.concatenate(pieces_out, axis=0)  5.7 us
    ppermute x1, starting transfers between devices, passed_along(): lax.ppermute(value, axis, [(source, source + steps) for source in range(l...  4.96 us
  transfers between devices with their start and end apart: 3, of which 2 were waited for; matrix products, arithmetic and copies ran while one was open for 12% of the time, Pallas kernels for 0%

commit v1 on v0

--- a/solution.py
+++ b/solution.py
@@ -136,7 +136,9 @@
         jnp.float32
     )
     gated = ssd_out.reshape(tok_rows, channels) * silu_act(z_gate.astype(jnp.float32))
-    square_sum = lax.psum(jnp.sum(gated * gated, axis=1), "tensor")
+    z_in = jnp.sum(gated * gated, axis=1)
+    back = jax.lax.all_gather(z_in, "tensor")
+    square_sum = jnp.sum(back, axis=0)
     width_all = channels * lax.axis_size("tensor")
     mixed_seq = (
         gated * lax.rsqrt(square_sum / width_all + EPSILON)[:, None] * norm_gain[None, :]

time: 158 us -> 158 us (level)
    psum x1 -> x0, blocking collectives: 6.37 us -> none  [local(): square_sum = lax.psum(jnp.sum(gated * gated, axis=1), 'tensor')]
    all_gather x0 -> x1, blocking collectives: none -> 5.18 us  [local(): back = jax.lax.all_gather(z_in, 'tensor')]
    reduce_sum x1 -> x2, other arithmetic: 4.24 us -> 4.27 us  [the longest x1 4.24 us: local(): z_in = jnp.sum(gated * gated, axis=1)]
where the time goes in v1:
time: 158 us; the launch traced here: 157 us
  waiting for transfers between devices  67.9 us (43%)
  other arithmetic  20.1 us (13%)
  local copies, waits for them, and re-layouts  18.7 us (12%)
  blocking collectives  15.3 us (10%)
  between operations  15.1 us (10%)
  matrix products  14.5 us (9%)
  starting transfers between devices  5.04 us (3%)
    all_gather x1, waiting for transfers between devices, local(): piece = lax.all_gather(summaries, 'seq', axis=0, tiled=True)  34.9 us
    all_gather x1, waiting for transfers between devices, prefix(): gathered = jax.tree.map(lambda a: lax.all_gather(a, axis), part)  33 us
    unnamed x1, blocking collectives  10.1 us
    dot_general x2, matrix products, stretch_local(): jnp.einsum('hij,jhp->ihp', mixing, x_block, preferred_element_type=jnp.fl...  6.59 us
    convert_element_type x2, other arithmetic, causal_conv(): return silu_act(summed).astype(jnp.bfloat16)  5.91 us
    concatenate x2, local copies, waits for them, and re-layouts, local(): jnp.concatenate(pieces_out, axis=0)  5.7 us
    all_gather x1, blocking collectives, local(): back = jax.lax.all_gather(z_in, 'tensor')  5.18 us
    ppermute x1, starting transfers between devices, passed_along(): lax.ppermute(value, axis, [(source, source + steps) for source in range(l...  4.96 us
  transfers between devices with their start and end apart: 3, of which 2 were waited for; matrix products, arithmetic and copies ran while one was open for 12% of the time, Pallas kernels for 0%

profile of v1, /device:TPU:0, one launch (start us, length us, event | category | flops | bytes accessed | tf_op | source)
XLA Modules:
  0.0 156.7 jit_solution(1446903970156979110)
XLA Ops:
  7.2 0.7 slice.120
  7.9 0.7 slice.121
  8.7 5.0 %collective-permute-start = (bf16[3,1536]{1,0:T(4,128)(2,1)S(1)}, bf16[3,1536]{1,0:T(4,128)(2,1)S(1)}, u32[]{:S(2)}, u32[]{:S(2)}) collective-permute-start(bf16[3,1536]{1,0:T(4,128)(2,1)S(1)} %pad_maximum_fusion.2), channel_id=1, source_target_pairs={{0,4},{4,8},{8,12},{1,5},{5,9},{9,13},{2,6},{6,10},{10,14},{3,7},{... | collective-permute-start | bytes 27656 | tf_op jit(solution)/shard_map/ppermute | solution.py:16
  13.6 0.8 fusion.71
  14.4 0.6 reduce-window.14
  15.4 0.6 reduce-window.16
  16.3 0.8 slice_convert_fusion.3
  17.2 0.8 slice_reduce_fusion.2
  17.9 0.5 fusion.72
  18.5 1.5 fusion.70
  19.9 0.9 convert_reduce_fusion.3
  20.8 0.6 exp.65
  21.5 4.0 %divide_convert_fusion = bf16[512,1280]{1,0:T(8,128)(2,1)S(1)} fusion(bf16[512,1280]{1,0:T(8,128)(2,1)} %param.15, bf16[3,1280]{1,0:T(4,128)(2,1)S(1)} %slice.158, f32[1280]{0:T(1024)S(1)} %get-tuple-element.52, f32[1280]{0:T(1024)S(1)} %get-tuple-element.53, f32[1280]{0:T(1024)S(1)} %get-tuple-element.51, f32[1280]{0:T(1024)S(1)} %get-tuple-element.50), kind=kLoop, calls=%fused_computation.25 | loop fusion | flops 15728640 | bytes 2649600 | tf_op jit(solution)/shard_map/convert_element_type | solution.py:45
  25.6 0.2 copy.34
  25.8 0.2 copy.39
  26.1 1.9 %divide_convert_fusion.1 = bf16[512,256]{1,0:T(8,128)(2,1)S(1)} fusion(bf16[512,256]{1,0:T(8,128)(2,1)} %param.17, bf16[3,256]{1,0:T(4,128)(2,1)S(1)} %slice.165, f32[256]{0:T(256)S(1)} %bitcast.92, f32[256]{0:T(256)S(1)} %bitcast.93, f32[256]{0:T(256)S(1)} %bitcast.91, f32[256]{0:T(256)S(1)} %bitcast.90), kind=kLoop, calls=%fused_computation.59 | loop fusion | flops 3145728 | bytes 529920 | tf_op jit(solution)/shard_map/convert_element_type | solution.py:45
  28.0 1.1 convolution_add_fusion.3
  29.1 1.9 %convolution_add_fusion.2 = f32[20,64,128]{2,1,0:T(8,128)} fusion(bf16[256,20,64]{0,2,1:T(8,128)(2,1)S(1)} %bitcast.76, f32[256,20]{0,1:T(8,128)} %get-tuple-element.72, f32[20,64,128]{2,1,0:T(8,128)S(1)} %convolution_add_fusion.3, f32[20]{0:T(128)} %exp.65, bf16[512,256]{1,0:T(8,128)(2,1)S(1)} %divide_convert_fusion.1), kind=kOutput, calls=%fused_computation.43 | convolution fusion | flops 85196800 | bytes 2052176 | tf_op jit(solution)/shard_map/jhp,js->hps/dot_general | solution.py:61
  31.1 1.2 dynamic-slice
  33.0 0.9 dynamic-update-slice
  33.8 10.1 %all-reduce = f32[80]{0:T(128)S(1)} all-reduce(f32[80]{0:T(128)S(1)} %dynamic-update-slice), channel_id=2, replica_groups=mesh['groups'=2,'seq'=4,'tensor'=4] {'seq'}, use_global_device_ids=true, to_apply=%add | all-reduce | flops 80 | bytes 640
  44.1 0.7 mul.319
  44.8 0.7 mul.320
  45.4 0.7 compare_and_fusion
  46.5 3.7 %fusion.18 = f32[256,20,64]{0,2,1:T(8,128)} fusion(bf16[256,20,64]{0,2,1:T(8,128)(2,1)S(1)} %bitcast.79, f32[20,256]{1,0:T(8,128)} %get-tuple-element.70, f32[256,256]{1,0:T(8,128)S(1)} %fusion.57, f32[20,256]{1,0:T(8,128)} %bitcast.82, pred[256,256]{1,0:T(8,128)(4,1)S(1)} %iota_compare_fusion), kind=kOutput, calls=%fused_computation.31 | convolution fusion | flops 175636480 | bytes 2334720 | tf_op jit(solution)/shard_map/hij,jhp->ihp/dot_general | solution.py:58
  50.3 2.9 %fusion.17 = f32[256,20,64]{0,2,1:T(8,128)} fusion(bf16[256,20,64]{0,2,1:T(8,128)(2,1)S(1)} %bitcast.77, f32[20,256]{1,0:T(8,128)S(1)} %copy-done.11, f32[256,256]{1,0:T(8,128)S(1)} %fusion.53, f32[20,256]{1,0:T(8,128)S(1)} %bitcast.85, pred[256,256]{1,0:T(8,128)(4,1)S(1)} %iota_compare_fusion), kind=kOutput, calls=%fused_computation.30 | convolution fusion | flops 175636480 | bytes 2334720 | tf_op jit(solution)/shard_map/hij,jhp->ihp/dot_general | solution.py:58
  53.1 33.0 %all-gather.9.cloned.1.call-done = f32[80,64,128]{2,1,0:T(8,128)} async-done(((f32[20,64,128]{2,1,0:T(8,128)}), f32[80,64,128]{2,1,0:T(8,128)}) %all-gather.9.cloned.1.call-update) | async-done | bytes 2621456 | tf_op jit(solution)/shard_map/all_gather | solution.py:21
  86.3 0.3 fusion.44
  86.6 0.4 copy-done.9
  87.0 0.6 copy-done.3
  87.6 1.4 fusion.21
  89.0 2.8 %copy.40 = f32[256,1280]{1,0:T(8,128)} copy(f32[256,1280]{0,1:T(8,128)} %bitcast.74) | data formatting | bytes 2621440 | tf_op jit(solution)/shard_map/concatenate | solution.py:135
  91.8 0.4 fusion.41
  92.2 0.9 copy-done.2
  93.1 1.4 fusion.22
  94.6 2.9 %copy.41 = f32[256,1280]{1,0:T(8,128)} copy(f32[256,1280]{0,1:T(8,128)} %bitcast.73) | data formatting | bytes 2621440 | tf_op jit(solution)/shard_map/concatenate | solution.py:135
  97.5 4.2 %multiply_reduce_fusion = (f32[512]{0:T(512)S(1)}, f32[512,1280]{1,0:T(8,128)}) fusion(bf16[512,1280]{1,0:T(8,128)(2,1)} %param.16, bf16[512,1280]{1,0:T(8,128)(2,1)S(1)} %divide_convert_fusion, f32[1280]{0:T(1024)S(1)} %copy-done.10, f32[256,1280]{1,0:T(8,128)} %copy.41, f32[256,1280]{1,0:T(8,128)S(1)} %copy-done.1), kind=kLoop, calls=%fused_computation.14 | loop fusion | flops 7208448 | bytes 7871488 | tf_op jit(solution)/shard_map/reduce_sum | solution.py:139
  101.7 5.2 %all-gather.3 = f32[4,1,512]{2,1,0:T(1,128)S(1)} all-gather(f32[1,1,512]{2,1,0:T(1,128)S(1)} %bitcast.88), channel_id=4, replica_groups=mesh['groups'=2,'seq'=4,'tensor'=4] {'tensor'}, dimensions={0}, use_global_device_ids=true | all-gather | bytes 10240 | tf_op jit(solution)/shard_map/all_gather | solution.py:140
  107.0 2.0 %multiply_convert_fusion.4 = bf16[512,1280]{1,0:T(8,128)(2,1)S(1)} fusion(f32[512,1280]{1,0:T(8,128)} %get-tuple-element.67, f32[1280]{0:T(1024)S(1)} %copy-done.12, f32[512]{0:T(512)S(1)} %add_rsqrt_fusion), kind=kLoop, calls=%fused_computation.13 | loop fusion | flops 1966080 | bytes 3939328 | tf_op jit(solution)/shard_map/convert_element_type | solution.py:145
  109.0 0.9 gather_fusion
  109.9 0.8 broadcast_select_fusion
  110.8 0.2 reshape.196
  111.1 34.9 %all-gather.7.cloned.1.call-done = bf16[512,1280]{1,0:T(8,128)(2,1)} async-done(((bf16[128,1280]{1,0:T(8,128)(2,1)}), bf16[512,1280]{1,0:T(8,128)(2,1)}) %all-gather.7.cloned.1.call-update) | async-done | bytes 1310736 | tf_op jit(solution)/shard_map/all_gather | solution.py:153
  146.0 1.6 %copy.42 = bf16[512,1280]{0,1:T(8,128)(2,1)S(1)} copy(bf16[512,1280]{1,0:T(8,128)(2,1)} %all-gather.7.cloned.1.call-done) | data formatting | bytes 2621440 | tf_op jit(solution)/shard_map/all_gather | solution.py:153
  147.6 0.4 fusion.73
  148.0 0.3 fusion.31
  148.3 0.6 fusion.28
  149.0 0.8 reshape.197
  (69 shorter events, 1.8 us)
Async XLA Ops:
  7.2 79.0 %all-gather.9.cloned.1.call-start = ((), (), s32[]{:S(2)}) async-start(), calls=%async_computation.1 | async-start | bytes 3276800 | tf_op jit(solution)/shard_map/all_gather | solution.py:21
  8.7 12.8 %collective-permute-start = (bf16[3,1536]{1,0:T(4,128)(2,1)S(1)}, bf16[3,1536]{1,0:T(4,128)(2,1)S(1)}, u32[]{:S(2)}, u32[]{:S(2)}) collective-permute-start(bf16[3,1536]{1,0:T(4,128)(2,1)S(1)} %pad_maximum_fusion.2), channel_id=1, source_target_pairs={{0,4},{4,8},{8,12},{1,5},{5,9},{9,13},{2,6},{6,10},{10,14},{3,7},{... | collective-permute-start | bytes 27656 | tf_op jit(solution)/shard_map/ppermute | solution.py:16
  15.3 6.1 %copy-start.4 = (f32[3,8,2,128]{3,1,2,0:T(8,128)}, f32[3,8,2,128]{3,1,2,0:T(8,128)S(1)}, u32[]{:S(2)}) copy-start(f32[3,8,2,128]{3,1,2,0:T(8,128)S(1)} %copy.45) | copy-start | bytes 73732
  16.3 5.1 %copy-start.5 = (f32[3,8,2,128]{3,1,2,0:T(8,128)}, f32[3,8,2,128]{3,1,2,0:T(8,128)S(1)}, u32[]{:S(2)}) copy-start(f32[3,8,2,128]{3,1,2,0:T(8,128)S(1)} %copy.46) | copy-start | bytes 73732
  31.0 115.0 %all-gather.7.cloned.1.call-start = ((), (), s32[]{:S(2)}) async-start(), calls=%async_computation | async-start | bytes 1638400 | tf_op jit(solution)/shard_map/all_gather | solution.py:153
  46.5 3.7 %copy-start.6 = (f32[3,8,2,128]{3,1,2,0:T(8,128)S(1)}, f32[3,8,2,128]{3,1,2,0:T(8,128)}, u32[]{:S(2)}) copy-start(f32[3,8,2,128]{3,1,2,0:T(8,128)} %copy-done.5) | copy-start | bytes 73732
  46.5 3.7 %copy-start.11 = (f32[20,256]{1,0:T(8,128)S(1)}, f32[20,256]{1,0:T(8,128)}, u32[]{:S(2)}) copy-start(f32[20,256]{1,0:T(8,128)} %get-tuple-element.73) | copy-start | bytes 61444
  86.3 0.7 copy-start.9
  86.3 1.3 copy-start.3
  87.6 4.2 %copy-start.13 = (f32[20]{0:T(128)S(1)}, f32[20]{0:T(128)}, u32[]{:S(2)}) copy-start(f32[20]{0:T(128)} %get-tuple-element.84) | copy-start | bytes 244
  89.0 3.2 %copy-start.8 = (f32[256,20]{0,1:T(8,128)S(1)}, f32[256,20]{0,1:T(8,128)}, u32[]{:S(2)}) copy-start(f32[256,20]{0,1:T(8,128)} %get-tuple-element.76) | copy-start | bytes 61444
  91.8 1.3 copy-start.2
  94.6 2.9 %copy-start.1 = (f32[256,1280]{1,0:T(8,128)S(1)}, f32[256,1280]{1,0:T(8,128)}, u32[]{:S(2)}) copy-start(f32[256,1280]{1,0:T(8,128)} %copy.40) | copy-start | bytes 3932164
  94.6 2.9 %copy-start.10 = (f32[1280]{0:T(1024)S(1)}, f32[1280]{0:T(1024)}, u32[]{:S(2)}) copy-start(f32[1280]{0:T(1024)} %mul.320) | copy-start | bytes 15364
  97.5 9.5 %copy-start.12 = (f32[1280]{0:T(1024)S(1)}, f32[1280]{0:T(1024)}, u32[]{:S(2)}) copy-start(f32[1280]{0:T(1024)} %param.23) | copy-start | bytes 15364
  109.0 38.6 %copy-start = (bf16[512,1280]{1,0:T(8,128)(2,1)}, bf16[512,1280]{1,0:T(8,128)(2,1)S(1)}, u32[]{:S(2)}) copy-start(bf16[512,1280]{1,0:T(8,128)(2,1)S(1)} %multiply_convert_fusion.4) | copy-start | bytes 3932164
  109.0 1.8 %copy-start.7 = (bf16[40,1280]{1,0:T(8,128)(2,1)S(1)}, bf16[40,1280]{1,0:T(8,128)(2,1)}, u32[]{:S(2)}) copy-start(bf16[40,1280]{1,0:T(8,128)(2,1)} %param.25) | copy-start | bytes 307204
  109.0 2.0 %copy-start.14 = (s32[40]{0:T(128)S(1)}, s32[40]{0:T(128)}, u32[]{:S(2)}) copy-start(s32[40]{0:T(128)} %param.27) | copy-start | bytes 484
  109.0 2.0 %copy-start.15 = (s32[40]{0:T(128)S(1)}, s32[40]{0:T(128)}, u32[]{:S(2)}) copy-start(s32[40]{0:T(128)} %param.26) | copy-start | bytes 484
Sparse Core Ops, SparseCore 0:
  31.1 55.0 all-gather.8
  110.9 35.0 all-gather.6
